TPU v7x, 128 devices: a whole 4x4x4 slice. The times are simulated.
128 devices in a mesh: gx: 16 (over z, x), gy: 8 (over y, core).
Axes of the slice: x: 4, y: 4, z: 4, core: 2. Of those that a mesh axis runs over, the one named last changes fastest.
Arguments:
- parent_field: float32 [8, 2048, 4096], P(None, 'gx', 'gy'), may hold values from -6 to 6
- parent_sppt: bfloat16 [2048, 4096], P('gx', 'gy'), may hold values from -0.796875 to 0.796875
- child_storm: float32 [8, 2048, 3072], P(None, 'gx', 'gy'), may hold values from -6 to 6
- child_sppt: bfloat16 [2048, 3072], P('gx', 'gy'), may hold values from -0.796875 to 0.796875
- wind: float32 [2, 8], replicated, may hold values from -0.3 to 0.3
- strip_dest: int32 [16384, 1], replicated, may hold values from 0 to 127; in each aligned block of 128 rows (0 to 127, 128 to 255, ...) at most 2 rows name the same one
- strip_row: int32 [16384], replicated, may hold values from 0 to 511
- strip_target: int32 [16384], replicated, may hold values from 0 to 127
- storm_shift: int32 [2, 4], replicated, may hold values from 0 to 15, as said below
Outputs:
- new_parent: float32 [8, 2048, 4096], P(None, 'gx', 'gy')
- child: float32 [8, 2048, 3072], P(None, 'gx', 'gy')
Inputs may be any that keep to these rules, and one draw needn't show every extreme that they name: `strip_dest`: among the 128 strips of one parent device no owner appears more than 2 times. `storm_shift`: row 0 lies in 0 to 16 - 1 and holds 16 - 1 at least once; row 1 lies in 0 to 8 - 1 and holds 8 - 1 at least once.
All inputs are finite; a program needn't handle non-finite values.
Results may differ from a plain program's by a relative error of at most 0.0003.
Values sent between devices are 32-bit elements; how exact they have to be, the bound alone decides.
No kernel may reach another device: no remote copies, remote signals or barrier semaphores. Data moves between devices by JAX's collectives and lax.ppermute only.
A program may use at most 64 MiB of HBM per device.

v0:
```python
import jax
import jax.numpy as jnp
from jax import lax
from jax.sharding import PartitionSpec as P

SUBSTEPS = 3
STRIP = 128
CAP = 2
KAPPA = 0.1
VERTICAL = 0.1
NUDGE = 0.5


def edge_halos(block):

    def swap(edge, axis, forward):
        count = lax.axis_size(axis)
        pairs = [(i, i + 1) for i in range(count - 1)]
        if not forward:
            pairs = [(target, source) for source, target in pairs]
        return lax.ppermute(edge, axis, pairs)

    before_x = swap(block[:, -1, :], "gx", True)
    after_x = swap(block[:, 0, :], "gx", False)
    before_y = swap(block[:, :, -1], "gy", True)
    after_y = swap(block[:, :, 0], "gy", False)
    return (before_x, after_x, before_y, after_y)


def halo_tendency(block, wind_x, wind_y):
    before_x, after_x, before_y, after_y = edge_halos(block)
    north = jnp.concatenate([block[:, 1:, :], after_x[:, None, :]], axis=1)
    south = jnp.concatenate([before_x[:, None, :], block[:, :-1, :]], axis=1)
    east = jnp.concatenate([block[:, :, 1:], after_y[:, :, None]], axis=2)
    west = jnp.concatenate([before_y[:, :, None], block[:, :, :-1]], axis=2)
    laplace = north + south + east + west - 4.0 * block
    return KAPPA * laplace - wind_x * (0.5 * (north - south)) - wind_y * (0.5 * (east - west))


def from_behind(value, axis, steps):
    count = lax.axis_size(axis)
    pairs = [(source, (source + steps) % count) for source in range(count)]
    return lax.ppermute(value, axis, pairs)


def storm_rows(child, storm_shift, nx, ny):
    levels, crows, widths = child.shape
    mine = lax.axis_index(("gx", "gy"))
    gathered = lax.all_to_all(child, ("gx", "gy"), 1, 1, tiled=True)
    piece = mine // (crows // storm_shift.shape[1])
    grid = gathered.reshape(levels, nx, ny, widths)
    grid = jnp.roll(grid, storm_shift[0, piece], axis=1)
    grid = jnp.roll(grid, storm_shift[1, piece], axis=2)
    return lax.all_to_all(grid.reshape(levels, crows, widths), ("gx", "gy"), 1, 1, tiled=True)


def refine_table(strip):
    coarse = jnp.arange(strip).astype(jnp.float32)
    finer = jnp.arange(3 * strip).astype(jnp.float32)
    position = jnp.clip((finer + 0.5) / 3.0 - 0.5, 0.0, strip - 1.0)
    return jnp.maximum(0.0, 1.0 - jnp.abs(position[None, :] - coarse[:, None]))


def vertical(field):
    upper = jnp.concatenate([field[1:], field[-1:]], axis=0)
    lower = jnp.concatenate([field[:1], field[:-1]], axis=0)
    return upper + lower - 2.0 * field


def shards(
    parent_field,
    parent_sppt,
    child_storm,
    child_sppt,
    wind,
    strip_dest,
    strip_row,
    strip_target,
    storm_shift,
):
    devices = lax.axis_size(("gx", "gy"))
    my_index = lax.axis_index(("gx", "gy"))
    wind_x = wind[0][:, None, None]
    wind_y = wind[1][:, None, None]
    new_parent = parent_field + (1.0 + parent_sppt.astype(jnp.float32)) * (
        halo_tendency(parent_field, wind_x, wind_y) + VERTICAL * vertical(parent_field)
    )
    levels, crows, widths = child_storm.shape
    npiece = storm_shift.shape[1]
    band_rows = crows // npiece
    nx, ny = (lax.axis_size("gx"), lax.axis_size("gy"))
    child = storm_rows(child_storm, storm_shift, nx, ny)
    dest_table = strip_dest.reshape(devices, -1)
    row_table = strip_row.reshape(devices, -1)
    target_table = strip_target.reshape(devices, -1)
    slots = dest_table.shape[1]
    my_dest = lax.dynamic_index_in_dim(dest_table, my_index, 0, keepdims=False)
    my_rows = lax.dynamic_index_in_dim(row_table, my_index, 0, keepdims=False)
    same_owner = my_dest[:, None] == my_dest[None, :]
    earlier = jnp.arange(slots)[None, :] < jnp.arange(slots)[:, None]
    rank = jnp.sum((same_owner & earlier).astype(jnp.int32), axis=1)
    slot_index = my_dest * CAP + rank
    send_select = (jnp.arange(devices * CAP)[:, None] == slot_index[None, :]).astype(jnp.float32)
    both_states = jnp.stack([parent_field, new_parent]).reshape(2, levels, -1, STRIP)
    picked = jnp.take(both_states, my_rows, axis=2)
    strip_values = jnp.moveaxis(picked, 2, 0).reshape(slots, -1)
    outgoing_strips = jnp.dot(
        send_select,
        strip_values,
        precision=lax.Precision.HIGHEST,
        preferred_element_type=jnp.float32,
    )
    incoming = lax.all_to_all(
        outgoing_strips, ("gx", "gy"), split_axis=0, concat_axis=0, tiled=True
    )
    mine = dest_table == my_index
    rank_all = jnp.cumsum(mine.astype(jnp.int32), axis=1) - 1
    slot_ids = jnp.arange(CAP)
    hits = mine[:, None, :] & (rank_all[:, None, :] == slot_ids[None, :, None])
    chosen = jnp.sum(jnp.where(hits, target_table[:, None, :], 0), axis=2)
    target_rows = jnp.where(jnp.any(hits, axis=2), chosen, -1).reshape(-1)
    row_select = (jnp.arange(crows)[:, None] == target_rows[None, :]).astype(jnp.float32)
    coarse = jnp.dot(
        row_select, incoming, precision=lax.Precision.HIGHEST, preferred_element_type=jnp.float32
    )
    counts = jnp.sum(row_select, axis=1)
    boundary = jnp.einsum(
        "tald,de->alte",
        coarse.reshape(crows, 2, levels, STRIP),
        refine_table(STRIP),
        precision=lax.Precision.HIGHEST,
    )
    divisor = 1.0 + NUDGE * counts[None, :, None]
    factor = 1.0 + child_sppt.astype(jnp.float32)
    for substep in range(SUBSTEPS):
        weight = (substep + 1) / 3.0
        target_value = boundary[0] + weight * (boundary[1] - boundary[0])
        child = (
            child + factor * halo_tendency(child, wind_x, wind_y) + NUDGE * target_value
        ) / divisor
    return (new_parent, child)


def solution(mesh):
    placed = (
        P(None, "gx", "gy"),
        P("gx", "gy"),
        P(None, "gx", "gy"),
        P("gx", "gy"),
        P(),
        P(),
        P(),
        P(),
        P(),
    )
    return jax.shard_map(
        shards,
        mesh=mesh,
        in_specs=placed,
        out_specs=(P(None, "gx", "gy"), P(None, "gx", "gy")),
        check_vma=False,
    )
```

profile of v0, /device:TPU:40, one launch (start us, length us, event | category | flops | bytes accessed | tf_op | source)
XLA Modules:
  0.0 225.1 jit_solution(2498742965248244502)
XLA Ops:
  4.5 3.6 %collective-permute-start.2 = (f32[8,128]{1,0:T(8,128)S(1)}, f32[8,128]{1,0:T(8,128)S(1)}, u32[]{:S(2)}, u32[]{:S(2)}) collective-permute-start(f32[8,128]{1,0:T(8,128)S(1)} %bitcast.132), channel_id=1, source_target_pairs={{1,0},{2,1},{3,2},{4,3},{5,4},{6,5},{7,6},{9,8},{10,9},{11,10},{12... | collective-permute-start | bytes 12296 | tf_op jit(solution)/shard_map/ppermute | solution.py:21
  8.2 3.4 %collective-permute-start.1 = (f32[8,512]{1,0:T(8,128)S(1)}, f32[8,512]{1,0:T(8,128)S(1)}, u32[]{:S(2)}, u32[]{:S(2)}) collective-permute-start(f32[8,512]{1,0:T(8,128)S(1)} %bitcast.120), channel_id=1, source_target_pairs={{0,8},{8,16},{16,24},{24,32},{32,40},{40,48},{48,56},{56,64},{64,7... | collective-permute-start | bytes 49160 | tf_op jit(solution)/shard_map/ppermute | solution.py:21
  11.6 4.6 %collective-permute-start = (f32[8,512]{1,0:T(8,128)S(1)}, f32[8,512]{1,0:T(8,128)S(1)}, u32[]{:S(2)}, u32[]{:S(2)}) collective-permute-start(f32[8,512]{1,0:T(8,128)S(1)} %bitcast.122), channel_id=1, source_target_pairs={{8,0},{16,8},{24,16},{32,24},{40,32},{48,40},{56,48},{64,56},{72,6... | collective-permute-start | bytes 49160 | tf_op jit(solution)/shard_map/ppermute | solution.py:21
  16.2 3.5 %copy.138 = f32[8,128,384]{2,0,1:T(8,128)} copy(f32[8,128,384]{2,1,0:T(8,128)} %param.11) | data formatting | bytes 3145728 | tf_op args[2]
  19.7 8.5 %all-to-all-start = ((f32[8,128,384]{2,0,1:T(8,128)}), f32[8,128,384]{2,0,1:T(8,128)}, u32[]{:S(2)}, u32[]{:S(2)}) async-start(f32[8,128,384]{2,0,1:T(8,128)} %copy.138), calls=%async_computation | async-start | bytes 3145728 | tf_op jit(solution)/shard_map/all_to_all | solution.py:49
  41.3 4.2 %copy.155 = f32[1,8,512,128]{3,1,2,0:T(8,128)} copy(f32[1,8,512,128]{3,2,1,0:T(8,128)} %stack.9) | data formatting | bytes 4194304 | tf_op jit(solution)/shard_map/stack | solution.py:104
  47.3 7.0 %fusion.4 = f32[8,128,512]{2,1,0:T(8,128)} fusion(f32[8,128,512]{2,1,0:T(8,128)S(1)} %copy-done, f32[1,128,512]{2,1,0:T(8,128)} %get-tuple-element.27, f32[7,128,512]{2,1,0:T(8,128)} %get-tuple-element.29, f32[7,128,512]{2,1,0:T(8,128)} %get-tuple-element.28, f32[1,128,512]{2,1,0:T(8,128)} %get-tuple-element.26, f32[8,128,511]{2,1,0:T(8,128)} %get-tuple-element.23, ...), kind=kLoop, calls=%fused_computation.15 | loop fusion | flops 13107200 | bytes 17039424 | tf_op jit(solution)/shard_map/add | solution.py:85
  64.6 3.0 %copy.157 = f32[128,2,2048]{2,1,0:T(2,128)} copy(f32[128,2,2048]{2,0,1:T(8,128)S(1)} %fusion.19) | data formatting | bytes 4194304 | tf_op jit(solution)/shard_map/dot_general | solution.py:107
  67.5 9.8 %all-to-all-start.2 = ((f32[128,2,2048]{2,1,0:T(2,128)}), f32[128,2,2048]{2,1,0:T(2,128)S(1)}, u32[]{:S(2)}, u32[]{:S(2)}) async-start(f32[128,2,2048]{2,1,0:T(2,128)} %copy.157), calls=%async_computation.2 | async-start | bytes 4194304 | tf_op jit(solution)/shard_map/all_to_all | solution.py:113
  86.8 17.8 %all-to-all-done.2 = f32[128,2,2048]{2,1,0:T(2,128)S(1)} async-done(((f32[128,2,2048]{2,1,0:T(2,128)}), f32[128,2,2048]{2,1,0:T(2,128)S(1)}, u32[]{:S(2)}, u32[]{:S(2)}) %all-to-all-start.2) | async-done | bytes 2097184 | tf_op jit(solution)/shard_map/all_to_all | solution.py:113
  105.9 7.7 %all-to-all-start.1 = ((f32[8,128,384]{2,0,1:T(8,128)}), f32[8,128,384]{2,0,1:T(8,128)S(1)}, u32[]{:S(2)}, u32[]{:S(2)}) async-start(f32[8,128,384]{2,0,1:T(8,128)} %copy.140), calls=%async_computation.1 | async-start | bytes 3145728 | tf_op jit(solution)/shard_map/all_to_all | solution.py:54
  114.2 3.6 %all_to_all.15 = f32[256,2048]{1,0:T(8,128)} reshape(f32[128,2,2048]{2,1,0:T(2,128)} %copy-done.1) | data formatting | bytes 4194304 | tf_op jit(solution)/shard_map/all_to_all | solution.py:113
  123.5 4.4 %convolution_bitcast_fusion = f32[2,8,128,384]{2,3,1,0:T(8,128)} fusion(f32[128,2,8,128]{3,0,2,1:T(8,128)S(1)} %fusion.15, f32[128]{0:T(128)S(1)} %iota_convert_fusion, f32[384]{0:T(512)S(1)} %add_clamp_fusion), kind=kOutput, calls=%fused_computation.16 | convolution fusion | flops 1208156160 | bytes 4196352 | tf_op jit(solution)/shard_map/tald,de->alte/dot_general | solution.py:127
  127.9 7.3 %all-to-all-done.1 = f32[8,128,384]{2,0,1:T(8,128)S(1)} async-done(((f32[8,128,384]{2,0,1:T(8,128)}), f32[8,128,384]{2,0,1:T(8,128)S(1)}, u32[]{:S(2)}, u32[]{:S(2)}) %all-to-all-start.1) | async-done | bytes 1572896 | tf_op jit(solution)/shard_map/all_to_all | solution.py:54
  143.3 3.9 %collective-permute-start.6 = (f32[8,128]{1,0:T(8,128)S(1)}, f32[8,128]{1,0:T(8,128)S(1)}, u32[]{:S(2)}, u32[]{:S(2)}) collective-permute-start(f32[8,128]{1,0:T(8,128)S(1)} %bitcast.141), channel_id=1, source_target_pairs={{1,0},{2,1},{3,2},{4,3},{5,4},{6,5},{7,6},{9,8},{10,9},{11,10},{12... | collective-permute-start | bytes 12296 | tf_op jit(solution)/shard_map/ppermute | solution.py:21
  149.9 5.4 %collective-permute-start.4 = (f32[8,384]{1,0:T(8,128)S(1)}, f32[8,384]{1,0:T(8,128)S(1)}, u32[]{:S(2)}, u32[]{:S(2)}) collective-permute-start(f32[8,384]{1,0:T(8,128)S(1)} %get-tuple-element.44), channel_id=1, source_target_pairs={{8,0},{16,8},{24,16},{32,24},{40,32},{48,40},{56,48},{64,56},{72,6... | collective-permute-start | bytes 36872 | tf_op jit(solution)/shard_map/ppermute | solution.py:21
  160.9 5.5 %add_divide_fusion.2 = f32[8,128,384]{1,2,0:T(8,128)S(1)} fusion(f32[8,128,384]{1,2,0:T(8,128)S(1)} %copy.151, f32[8,128,383]{1,2,0:T(8,128)} %get-tuple-element.47, f32[8,128,1]{1,2,0:T(1,128)S(1)} %bitcast.134, f32[8,128,1]{1,2,0:T(1,128)S(1)} %bitcast.137, f32[8,128,383]{1,2,0:T(8,128)} %get-tuple-element.46, f32[8,127,384]{1,2,0:T(8,128)} %get-tuple-element.43, ...), kind=kLoop, calls=%fused_computation.42 | loop fusion | flops 9437184 | bytes 12780096 | tf_op jit(solution)/shard_map/div | solution.py:138
  171.6 3.6 %collective-permute-start.10 = (f32[8,128]{1,0:T(8,128)S(1)}, f32[8,128]{1,0:T(8,128)S(1)}, u32[]{:S(2)}, u32[]{:S(2)}) collective-permute-start(f32[8,128]{1,0:T(8,128)S(1)} %bitcast.142), channel_id=1, source_target_pairs={{1,0},{2,1},{3,2},{4,3},{5,4},{6,5},{7,6},{9,8},{10,9},{11,10},{12... | collective-permute-start | bytes 12296 | tf_op jit(solution)/shard_map/ppermute | solution.py:21
  177.2 6.0 %collective-permute-start.8 = (f32[8,384]{1,0:T(8,128)S(1)}, f32[8,384]{1,0:T(8,128)S(1)}, u32[]{:S(2)}, u32[]{:S(2)}) collective-permute-start(f32[8,384]{1,0:T(8,128)S(1)} %get-tuple-element.14), channel_id=1, source_target_pairs={{8,0},{16,8},{24,16},{32,24},{40,32},{48,40},{56,48},{64,56},{72,6... | collective-permute-start | bytes 36872 | tf_op jit(solution)/shard_map/ppermute | solution.py:21
  188.8 5.5 %add_divide_fusion.1 = f32[8,128,384]{1,2,0:T(8,128)S(1)} fusion(f32[8,128,384]{1,2,0:T(8,128)S(1)} %add_divide_fusion.2, f32[8,128,383]{1,2,0:T(8,128)} %get-tuple-element.39, f32[8,128,1]{1,2,0:T(1,128)S(1)} %bitcast.138, f32[8,128,1]{1,2,0:T(1,128)S(1)} %bitcast.140, f32[8,128,383]{1,2,0:T(8,128)} %get-tuple-element.38, ...), kind=kLoop, calls=%fused_computation.41 | loop fusion | flops 9437184 | bytes 12780096 | tf_op jit(solution)/shard_map/div | solution.py:138
  198.9 3.6 %collective-permute-start.14 = (f32[8,128]{1,0:T(8,128)S(1)}, f32[8,128]{1,0:T(8,128)S(1)}, u32[]{:S(2)}, u32[]{:S(2)}) collective-permute-start(f32[8,128]{1,0:T(8,128)S(1)} %bitcast.143), channel_id=1, source_target_pairs={{1,0},{2,1},{3,2},{4,3},{5,4},{6,5},{7,6},{9,8},{10,9},{11,10},{12... | collective-permute-start | bytes 12296 | tf_op jit(solution)/shard_map/ppermute | solution.py:21
  204.5 6.0 %collective-permute-start.12 = (f32[8,384]{1,0:T(8,128)S(1)}, f32[8,384]{1,0:T(8,128)S(1)}, u32[]{:S(2)}, u32[]{:S(2)}) collective-permute-start(f32[8,384]{1,0:T(8,128)S(1)} %get-tuple-element.12), channel_id=1, source_target_pairs={{8,0},{16,8},{24,16},{32,24},{40,32},{48,40},{56,48},{64,56},{72,6... | collective-permute-start | bytes 36872 | tf_op jit(solution)/shard_map/ppermute | solution.py:21
  216.2 5.9 %add_divide_fusion = f32[8,128,384]{1,2,0:T(8,128)} fusion(f32[8,128,384]{1,2,0:T(8,128)S(1)} %add_divide_fusion.1, f32[8,128,383]{1,2,0:T(8,128)} %get-tuple-element.33, f32[8,128,1]{1,2,0:T(1,128)S(1)} %bitcast.135, f32[8,128,1]{1,2,0:T(1,128)S(1)} %bitcast.136, f32[8,128,383]{1,2,0:T(8,128)S(1)} %get-tuple-element.32, ...), kind=kLoop, calls=%fused_computation.40 | loop fusion | flops 9043968 | bytes 12780096 | tf_op jit(solution)/shard_map/div | solution.py:138
  222.1 3.0 %copy.168 = f32[8,128,384]{2,1,0:T(8,128)} copy(f32[8,128,384]{1,2,0:T(8,128)} %add_divide_fusion) | data formatting | bytes 3145728
  (125 shorter events, 83.3 us)
Async XLA Ops:
  0.6 7.5 %copy-start = (f32[8,128,512]{2,1,0:T(8,128)S(1)}, f32[8,128,512]{2,1,0:T(8,128)}, u32[]{:S(2)}) copy-start(f32[8,128,512]{2,1,0:T(8,128)} %param.9) | copy-start | bytes 6291460
  2.4 43.1 %collective-permute-start.3 = (f32[8,128]{1,0:T(8,128)S(1)}, f32[8,128]{1,0:T(8,128)S(1)}, u32[]{:S(2)}, u32[]{:S(2)}) collective-permute-start(f32[8,128]{1,0:T(8,128)S(1)} %bitcast.130), channel_id=1, source_target_pairs={{0,1},{1,2},{2,3},{3,4},{4,5},{5,6},{6,7},{8,9},{9,10},{10,11},{11... | collective-permute-start | bytes 12296 | tf_op jit(solution)/shard_map/ppermute | solution.py:21
  4.5 41.3 %collective-permute-start.2 = (f32[8,128]{1,0:T(8,128)S(1)}, f32[8,128]{1,0:T(8,128)S(1)}, u32[]{:S(2)}, u32[]{:S(2)}) collective-permute-start(f32[8,128]{1,0:T(8,128)S(1)} %bitcast.132), channel_id=1, source_target_pairs={{1,0},{2,1},{3,2},{4,3},{5,4},{6,5},{7,6},{9,8},{10,9},{11,10},{12... | collective-permute-start | bytes 12296 | tf_op jit(solution)/shard_map/ppermute | solution.py:21
  8.2 39.1 %collective-permute-start.1 = (f32[8,512]{1,0:T(8,128)S(1)}, f32[8,512]{1,0:T(8,128)S(1)}, u32[]{:S(2)}, u32[]{:S(2)}) collective-permute-start(f32[8,512]{1,0:T(8,128)S(1)} %bitcast.120), channel_id=1, source_target_pairs={{0,8},{8,16},{16,24},{24,32},{32,40},{40,48},{48,56},{56,64},{64,7... | collective-permute-start | bytes 49160 | tf_op jit(solution)/shard_map/ppermute | solution.py:21
  11.6 35.7 %collective-permute-start = (f32[8,512]{1,0:T(8,128)S(1)}, f32[8,512]{1,0:T(8,128)S(1)}, u32[]{:S(2)}, u32[]{:S(2)}) collective-permute-start(f32[8,512]{1,0:T(8,128)S(1)} %bitcast.122), channel_id=1, source_target_pairs={{8,0},{16,8},{24,16},{32,24},{40,32},{48,40},{56,48},{64,56},{72,6... | collective-permute-start | bytes 49160 | tf_op jit(solution)/shard_map/ppermute | solution.py:21
  19.7 47.9 %all-to-all-start = ((f32[8,128,384]{2,0,1:T(8,128)}), f32[8,128,384]{2,0,1:T(8,128)}, u32[]{:S(2)}, u32[]{:S(2)}) async-start(f32[8,128,384]{2,0,1:T(8,128)} %copy.138), calls=%async_computation | async-start | bytes 3145728 | tf_op jit(solution)/shard_map/all_to_all | solution.py:49
  34.2 3.3 %copy-start.5 = (s32[16384,1]{0,1:T(1,128)S(1)}, s32[16384,1]{0,1:T(1,128)}, u32[]{:S(2)}) copy-start(s32[16384,1]{0,1:T(1,128)} %param.14) | copy-start | bytes 196612
  67.5 9.8 %copy-start.11 = (s32[2,4]{1,0:T(2,128)S(1)}, s32[2,4]{1,0:T(2,128)}, u32[]{:S(2)}) copy-start(s32[2,4]{1,0:T(2,128)} %param.17) | copy-start | bytes 100
  67.5 14.6 %copy-start.6 = (s32[16384]{0:T(1024)S(1)}, s32[16384]{0:T(1024)}, u32[]{:S(2)}) copy-start(s32[16384]{0:T(1024)} %param.16) | copy-start | bytes 196612
  67.5 37.1 %all-to-all-start.2 = ((f32[128,2,2048]{2,1,0:T(2,128)}), f32[128,2,2048]{2,1,0:T(2,128)S(1)}, u32[]{:S(2)}, u32[]{:S(2)}) async-start(f32[128,2,2048]{2,1,0:T(2,128)} %copy.157), calls=%async_computation.2 | async-start | bytes 4194304 | tf_op jit(solution)/shard_map/all_to_all | solution.py:113
  86.8 27.1 %copy-start.4 = (bf16[128,384]{1,0:T(8,128)(2,1)S(1)}, bf16[128,384]{1,0:T(8,128)(2,1)}, u32[]{:S(2)}) copy-start(bf16[128,384]{1,0:T(8,128)(2,1)} %param.12) | copy-start | bytes 294916
  105.9 29.3 %all-to-all-start.1 = ((f32[8,128,384]{2,0,1:T(8,128)}), f32[8,128,384]{2,0,1:T(8,128)S(1)}, u32[]{:S(2)}, u32[]{:S(2)}) async-start(f32[8,128,384]{2,0,1:T(8,128)} %copy.140), calls=%async_computation.1 | async-start | bytes 3145728 | tf_op jit(solution)/shard_map/all_to_all | solution.py:54
  140.1 20.8 %collective-permute-start.7 = (f32[8,128]{1,0:T(8,128)S(1)}, f32[8,128]{1,0:T(8,128)S(1)}, u32[]{:S(2)}, u32[]{:S(2)}) collective-permute-start(f32[8,128]{1,0:T(8,128)S(1)} %bitcast.139), channel_id=1, source_target_pairs={{0,1},{1,2},{2,3},{3,4},{4,5},{5,6},{6,7},{8,9},{9,10},{10,11},{11... | collective-permute-start | bytes 12296 | tf_op jit(solution)/shard_map/ppermute | solution.py:21
  143.3 17.7 %collective-permute-start.6 = (f32[8,128]{1,0:T(8,128)S(1)}, f32[8,128]{1,0:T(8,128)S(1)}, u32[]{:S(2)}, u32[]{:S(2)}) collective-permute-start(f32[8,128]{1,0:T(8,128)S(1)} %bitcast.141), channel_id=1, source_target_pairs={{1,0},{2,1},{3,2},{4,3},{5,4},{6,5},{7,6},{9,8},{10,9},{11,10},{12... | collective-permute-start | bytes 12296 | tf_op jit(solution)/shard_map/ppermute | solution.py:21
  147.1 10.4 %collective-permute-start.5 = (f32[8,384]{1,0:T(8,128)S(1)}, f32[8,384]{1,0:T(8,128)S(1)}, u32[]{:S(2)}, u32[]{:S(2)}) collective-permute-start(f32[8,384]{1,0:T(8,128)S(1)} %get-tuple-element.45), channel_id=1, source_target_pairs={{0,8},{8,16},{16,24},{24,32},{32,40},{40,48},{48,56},{56,64},{64,7... | collective-permute-start | bytes 36872 | tf_op jit(solution)/shard_map/ppermute | solution.py:21
  149.9 9.4 %collective-permute-start.4 = (f32[8,384]{1,0:T(8,128)S(1)}, f32[8,384]{1,0:T(8,128)S(1)}, u32[]{:S(2)}, u32[]{:S(2)}) collective-permute-start(f32[8,384]{1,0:T(8,128)S(1)} %get-tuple-element.44), channel_id=1, source_target_pairs={{8,0},{16,8},{24,16},{32,24},{40,32},{48,40},{56,48},{64,56},{72,6... | collective-permute-start | bytes 36872 | tf_op jit(solution)/shard_map/ppermute | solution.py:21
  169.7 19.1 %collective-permute-start.11 = (f32[8,128]{1,0:T(8,128)S(1)}, f32[8,128]{1,0:T(8,128)S(1)}, u32[]{:S(2)}, u32[]{:S(2)}) collective-permute-start(f32[8,128]{1,0:T(8,128)S(1)} %bitcast.144), channel_id=1, source_target_pairs={{0,1},{1,2},{2,3},{3,4},{4,5},{5,6},{6,7},{8,9},{9,10},{10,11},{11... | collective-permute-start | bytes 12296 | tf_op jit(solution)/shard_map/ppermute | solution.py:21
  171.6 17.2 %collective-permute-start.10 = (f32[8,128]{1,0:T(8,128)S(1)}, f32[8,128]{1,0:T(8,128)S(1)}, u32[]{:S(2)}, u32[]{:S(2)}) collective-permute-start(f32[8,128]{1,0:T(8,128)S(1)} %bitcast.142), channel_id=1, source_target_pairs={{1,0},{2,1},{3,2},{4,3},{5,4},{6,5},{7,6},{9,8},{10,9},{11,10},{12... | collective-permute-start | bytes 12296 | tf_op jit(solution)/shard_map/ppermute | solution.py:21
  175.2 10.1 %collective-permute-start.9 = (f32[8,384]{1,0:T(8,128)S(1)}, f32[8,384]{1,0:T(8,128)S(1)}, u32[]{:S(2)}, u32[]{:S(2)}) collective-permute-start(f32[8,384]{1,0:T(8,128)S(1)} %get-tuple-element.15), channel_id=1, source_target_pairs={{0,8},{8,16},{16,24},{24,32},{32,40},{40,48},{48,56},{56,64},{64,7... | collective-permute-start | bytes 36872 | tf_op jit(solution)/shard_map/ppermute | solution.py:21
  177.2 10.0 %collective-permute-start.8 = (f32[8,384]{1,0:T(8,128)S(1)}, f32[8,384]{1,0:T(8,128)S(1)}, u32[]{:S(2)}, u32[]{:S(2)}) collective-permute-start(f32[8,384]{1,0:T(8,128)S(1)} %get-tuple-element.14), channel_id=1, source_target_pairs={{8,0},{16,8},{24,16},{32,24},{40,32},{48,40},{56,48},{64,56},{72,6... | collective-permute-start | bytes 36872 | tf_op jit(solution)/shard_map/ppermute | solution.py:21
  197.0 19.2 %collective-permute-start.15 = (f32[8,128]{1,0:T(8,128)S(1)}, f32[8,128]{1,0:T(8,128)S(1)}, u32[]{:S(2)}, u32[]{:S(2)}) collective-permute-start(f32[8,128]{1,0:T(8,128)S(1)} %bitcast.145), channel_id=1, source_target_pairs={{0,1},{1,2},{2,3},{3,4},{4,5},{5,6},{6,7},{8,9},{9,10},{10,11},{11... | collective-permute-start | bytes 12296 | tf_op jit(solution)/shard_map/ppermute | solution.py:21
  198.9 17.3 %collective-permute-start.14 = (f32[8,128]{1,0:T(8,128)S(1)}, f32[8,128]{1,0:T(8,128)S(1)}, u32[]{:S(2)}, u32[]{:S(2)}) collective-permute-start(f32[8,128]{1,0:T(8,128)S(1)} %bitcast.143), channel_id=1, source_target_pairs={{1,0},{2,1},{3,2},{4,3},{5,4},{6,5},{7,6},{9,8},{10,9},{11,10},{12... | collective-permute-start | bytes 12296 | tf_op jit(solution)/shard_map/ppermute | solution.py:21
  202.6 10.2 %collective-permute-start.13 = (f32[8,384]{1,0:T(8,128)S(1)}, f32[8,384]{1,0:T(8,128)S(1)}, u32[]{:S(2)}, u32[]{:S(2)}) collective-permute-start(f32[8,384]{1,0:T(8,128)S(1)} %get-tuple-element.13), channel_id=1, source_target_pairs={{0,8},{8,16},{16,24},{24,32},{32,40},{40,48},{48,56},{56,64},{64,7... | collective-permute-start | bytes 36872 | tf_op jit(solution)/shard_map/ppermute | solution.py:21
  204.5 9.9 %collective-permute-start.12 = (f32[8,384]{1,0:T(8,128)S(1)}, f32[8,384]{1,0:T(8,128)S(1)}, u32[]{:S(2)}, u32[]{:S(2)}) collective-permute-start(f32[8,384]{1,0:T(8,128)S(1)} %get-tuple-element.12), channel_id=1, source_target_pairs={{8,0},{16,8},{24,16},{32,24},{40,32},{48,40},{56,48},{64,56},{72,6... | collective-permute-start | bytes 36872 | tf_op jit(solution)/shard_map/ppermute | solution.py:21
  (8 other events, 12.6 us)
where the time goes:
time: 226 us; the launch traced here: 225 us
  starting transfers between devices  80.4 us (36%)
  local copies, waits for them, and re-layouts  75.5 us (33%)
  other arithmetic  30.8 us (14%)
  waiting for transfers between devices  25.2 us (11%)
  matrix products  8.25 us (4%)
  between operations  4.92 us (2%)
    ppermute x16, starting transfers between devices, swap(): return lax.ppermute(edge, axis, pairs)  54.5 us
    all_to_all x1, waiting for transfers between devices, shards(): lax.all_to_all(outgoing_strips, ('gx', 'gy'), split_axis=0, concat_axis=0...  17.8 us
    div x3, other arithmetic, shards(): (child + factor * halo_tendency(child, wind_x, wind_y) + NUDGE * target_v...  16.9 us
    unnamed x34, local copies, waits for them, and re-layouts  12 us
    all_to_all x1, starting transfers between devices, shards(): lax.all_to_all(outgoing_strips, ('gx', 'gy'), split_axis=0, concat_axis=0...  9.77 us
    slice x4, local copies, waits for them, and re-layouts, halo_tendency(): north = jnp.concatenate([block[:, 1:, :], after_x[:, None, :]], axis=1)  9.01 us
    all_to_all x1, starting transfers between devices, storm_rows(): gathered = lax.all_to_all(child, ('gx', 'gy'), 1, 1, tiled=True)  8.47 us
    another operation x4, local copies, waits for them, and re-layouts, shards(): jnp.stack([parent_field, new_parent]).reshape(2, levels, -1, STRIP)  8.4 us
  transfers between devices with their start and end apart: 19, of which 2 were waited for; matrix products, arithmetic and copies ran while one was open for 34% of the time, Pallas kernels for 0%

commit v1 on v0

--- a/solution.py
+++ b/solution.py
@@ -51,7 +51,17 @@
     grid = gathered.reshape(levels, nx, ny, widths)
     grid = jnp.roll(grid, storm_shift[0, piece], axis=1)
     grid = jnp.roll(grid, storm_shift[1, piece], axis=2)
-    return lax.all_to_all(grid.reshape(levels, crows, widths), ("gx", "gy"), 1, 1, tiled=True)
+    return jnp.concatenate(
+        lax.all_to_all(
+            jnp.stack(
+                jnp.split(grid.reshape(levels, crows, widths), lax.axis_size(("gx", "gy")), axis=1)
+            ),
+            ("gx", "gy"),
+            0,
+            0,
+        ),
+        axis=1,
+    )
 
 
 def refine_table(strip):

time: 226 us -> 282 us (1.25)
  local copies, waits for them, and re-layouts: 75.5 us -> 146 us
  waiting for transfers between devices: 25.2 us -> 10.8 us
    unnamed x34 -> x147, local copies, waits for them, and re-layouts: 12 us -> 83.1 us
    all_to_all x1, waiting for transfers between devices: 17.8 us -> 0.01 us  [shards(): lax.all_to_all(outgoing_strips, ('gx', 'gy'), split_axis=0, concat_axis=0...]
    all_to_all x1, waiting for transfers between devices: 7.35 us -> 10.7 us  [storm_rows(): lax.all_to_all(jnp.stack(jnp.split(grid.reshape(levels, crows, widths), l...]
  transfers between devices with their start and end apart: 19 -> 19, of which waited for: 2 -> 1; matrix products, arithmetic and copies ran while one was open for 34% -> 52% of each run, Pallas kernels for 0% -> 0%
where the time goes in v1:
time: 282 us; the launch traced here: 281 us
  local copies, waits for them, and re-layouts  146 us (52%)
  starting transfers between devices  82.9 us (29%)
  other arithmetic  29.3 us (10%)
  waiting for transfers between devices  10.8 us (4%)
  matrix products  6.67 us (2%)
  between operations  5.29 us (2%)
    unnamed x147, local copies, waits for them, and re-layouts  83.1 us
    ppermute x16, starting transfers between devices, swap(): return lax.ppermute(edge, axis, pairs)  54.5 us
    div x3, other arithmetic, shards(): (child + factor * halo_tendency(child, wind_x, wind_y) + NUDGE * target_v...  16.9 us
    all_to_all x1, waiting for transfers between devices, storm_rows(): lax.all_to_all(jnp.stack(jnp.split(grid.reshape(levels, crows, widths), l...  10.7 us
    all_to_all x1, starting transfers between devices, storm_rows(): lax.all_to_all(jnp.stack(jnp.split(grid.reshape(levels, crows, widths), l...  10.2 us
    all_to_all x1, starting transfers between devices, shards(): lax.all_to_all(outgoing_strips, ('gx', 'gy'), split_axis=0, concat_axis=0...  9.77 us
    slice x4, local copies, waits for them, and re-layouts, halo_tendency(): north = jnp.concatenate([block[:, 1:, :], after_x[:, None, :]], axis=1)  8.97 us
    all_to_all x1, starting transfers between devices, storm_rows(): gathered = lax.all_to_all(child, ('gx', 'gy'), 1, 1, tiled=True)  8.48 us
  transfers between devices with their start and end apart: 19, of which 1 were waited for; matrix products, arithmetic and copies ran while one was open for 52% of the time, Pallas kernels for 0%

profile of v1, /device:TPU:40, one launch (start us, length us, event | category | flops | bytes accessed | tf_op | source)
XLA Modules:
  0.0 280.9 jit_solution(1669845772374963624)
XLA Ops:
  4.3 3.6 %collective-permute-start.2 = (f32[8,128]{1,0:T(8,128)S(1)}, f32[8,128]{1,0:T(8,128)S(1)}, u32[]{:S(2)}, u32[]{:S(2)}) collective-permute-start(f32[8,128]{1,0:T(8,128)S(1)} %get-tuple-element.70), channel_id=1, source_target_pairs={{1,0},{2,1},{3,2},{4,3},{5,4},{6,5},{7,6},{9,8},{10,9},{11,10},{12... | collective-permute-start | bytes 12296 | tf_op jit(solution)/shard_map/ppermute | solution.py:21
  8.9 3.4 %collective-permute-start.1 = (f32[8,512]{1,0:T(8,128)S(1)}, f32[8,512]{1,0:T(8,128)S(1)}, u32[]{:S(2)}, u32[]{:S(2)}) collective-permute-start(f32[8,512]{1,0:T(8,128)S(1)} %bitcast.752), channel_id=1, source_target_pairs={{0,8},{8,16},{16,24},{24,32},{32,40},{40,48},{48,56},{56,64},{64,7... | collective-permute-start | bytes 49160 | tf_op jit(solution)/shard_map/ppermute | solution.py:21
  12.3 4.6 %collective-permute-start = (f32[8,512]{1,0:T(8,128)S(1)}, f32[8,512]{1,0:T(8,128)S(1)}, u32[]{:S(2)}, u32[]{:S(2)}) collective-permute-start(f32[8,512]{1,0:T(8,128)S(1)} %bitcast.754), channel_id=1, source_target_pairs={{8,0},{16,8},{24,16},{32,24},{40,32},{48,40},{56,48},{64,56},{72,6... | collective-permute-start | bytes 49160 | tf_op jit(solution)/shard_map/ppermute | solution.py:21
  16.9 3.5 %copy.4947 = f32[8,128,384]{2,0,1:T(8,128)} copy(f32[8,128,384]{2,1,0:T(8,128)} %param.11) | data formatting | bytes 3145728 | tf_op args[2]
  20.4 8.5 %all-to-all-start = ((f32[8,128,384]{2,0,1:T(8,128)}), f32[8,128,384]{2,0,1:T(8,128)}, u32[]{:S(2)}, u32[]{:S(2)}) async-start(f32[8,128,384]{2,0,1:T(8,128)} %copy.4947), calls=%async_computation | async-start | bytes 3145728 | tf_op jit(solution)/shard_map/all_to_all | solution.py:49
  32.2 2.8 fusion.36
  45.9 4.2 %copy.4957 = f32[1,8,512,128]{3,1,2,0:T(8,128)} copy(f32[1,8,512,128]{3,2,1,0:T(8,128)} %stack.525) | data formatting | bytes 4194304 | tf_op jit(solution)/shard_map/stack | solution.py:114
  50.7 7.0 %fusion.4 = f32[8,128,512]{2,1,0:T(8,128)} fusion(f32[8,128,512]{2,1,0:T(8,128)S(1)} %copy-done, f32[1,128,512]{2,1,0:T(8,128)} %get-tuple-element.87, f32[7,128,512]{2,1,0:T(8,128)} %get-tuple-element.89, f32[7,128,512]{2,1,0:T(8,128)} %get-tuple-element.88, f32[1,128,512]{2,1,0:T(8,128)} %get-tuple-element.86, f32[8,128,511]{2,1,0:T(8,128)} %get-tuple-element.85, ...), kind=kLoop, calls=%fused_computation.15 | loop fusion | flops 13107200 | bytes 17039424 | tf_op jit(solution)/shard_map/add | solution.py:95
  63.1 2.9 %gather_fusion = f32[128,2,8,128]{3,2,1,0:T(8,128)S(1)} fusion(f32[2,8,512,128]{3,1,2,0:T(8,128)} %pad_maximum_fusion, s32[1024]{0:T(1024)S(1)} %pad_clamp_fusion), kind=kCustom, calls=%fused_computation | custom fusion | bytes 2097664 | tf_op jit(solution)/shard_map/jit(_take)/gather | solution.py:115
  67.4 2.9 %copy.4959 = f32[128,2,2048]{2,1,0:T(2,128)} copy(f32[128,2,2048]{2,0,1:T(8,128)S(1)} %fusion.18) | data formatting | bytes 4194304 | tf_op jit(solution)/shard_map/dot_general | solution.py:117
  70.4 9.8 %all-to-all-start.2 = ((f32[128,2,2048]{2,1,0:T(2,128)}), f32[128,2,2048]{2,1,0:T(2,128)S(1)}, u32[]{:S(2)}, u32[]{:S(2)}) async-start(f32[128,2,2048]{2,1,0:T(2,128)} %copy.4959), calls=%async_computation.2 | async-start | bytes 4194304 | tf_op jit(solution)/shard_map/all_to_all | solution.py:123
  160.5 10.2 %all-to-all-start.1 = ((f32[128,8,1,384]{3,1,2,0:T(8,128)}), f32[128,8,1,384]{3,1,2,0:T(8,128)}, u32[]{:S(2)}, u32[]{:S(2)}) async-start(f32[128,8,1,384]{3,1,2,0:T(8,128)} %constant_dynamic-update-slice_fusion), calls=%async_computation.1 | async-start | bytes 3145728 | tf_op jit(solution)/shard_map/all_to_all | solution.py:55
  176.9 4.4 %convolution_bitcast_fusion = f32[2,8,128,384]{2,3,1,0:T(8,128)} fusion(f32[128,2,8,128]{3,0,2,1:T(8,128)S(1)} %fusion.14, f32[128]{0:T(128)S(1)} %iota_convert_fusion, f32[384]{0:T(512)S(1)} %add_clamp_fusion), kind=kOutput, calls=%fused_computation.16 | convolution fusion | flops 1208156160 | bytes 4196352 | tf_op jit(solution)/shard_map/tald,de->alte/dot_general | solution.py:137
  181.3 10.7 %all-to-all-done.1 = f32[128,8,1,384]{3,1,2,0:T(8,128)} async-done(((f32[128,8,1,384]{3,1,2,0:T(8,128)}), f32[128,8,1,384]{3,1,2,0:T(8,128)}, u32[]{:S(2)}, u32[]{:S(2)}) %all-to-all-start.1) | async-done | bytes 1572896 | tf_op jit(solution)/shard_map/all_to_all | solution.py:55
  199.1 3.9 %collective-permute-start.6 = (f32[8,128]{1,0:T(8,128)S(1)}, f32[8,128]{1,0:T(8,128)S(1)}, u32[]{:S(2)}, u32[]{:S(2)}) collective-permute-start(f32[8,128]{1,0:T(8,128)S(1)} %bitcast.770), channel_id=1, source_target_pairs={{1,0},{2,1},{3,2},{4,3},{5,4},{6,5},{7,6},{9,8},{10,9},{11,10},{12... | collective-permute-start | bytes 12296 | tf_op jit(solution)/shard_map/ppermute | solution.py:21
  205.7 5.5 %collective-permute-start.4 = (f32[8,384]{1,0:T(8,128)S(1)}, f32[8,384]{1,0:T(8,128)S(1)}, u32[]{:S(2)}, u32[]{:S(2)}) collective-permute-start(f32[8,384]{1,0:T(8,128)S(1)} %get-tuple-element.76), channel_id=1, source_target_pairs={{8,0},{16,8},{24,16},{32,24},{40,32},{48,40},{56,48},{64,56},{72,6... | collective-permute-start | bytes 36872 | tf_op jit(solution)/shard_map/ppermute | solution.py:21
  216.7 5.5 %add_divide_fusion.2 = f32[8,128,384]{1,2,0:T(8,128)S(1)} fusion(f32[8,128,383]{1,2,0:T(8,128)} %get-tuple-element.105, f32[8,128,1]{1,2,0:T(1,128)S(1)} %bitcast.766, f32[8,128,1]{1,2,0:T(1,128)S(1)} %bitcast.768, f32[8,128,383]{1,2,0:T(8,128)} %get-tuple-element.104, f32[8,127,384]{1,2,0:T(8,128)} %get-tuple-element.103, f32[8,1,384]{1,2,0:T(8,128)} %copy.4953, ...), kind=kLoop, calls=%fused_computation.43 | loop fusion | flops 9437184 | bytes 12780096 | tf_op jit(solution)/shard_map/div | solution.py:148
  227.4 3.6 %collective-permute-start.10 = (f32[8,128]{1,0:T(8,128)S(1)}, f32[8,128]{1,0:T(8,128)S(1)}, u32[]{:S(2)}, u32[]{:S(2)}) collective-permute-start(f32[8,128]{1,0:T(8,128)S(1)} %bitcast.771), channel_id=1, source_target_pairs={{1,0},{2,1},{3,2},{4,3},{5,4},{6,5},{7,6},{9,8},{10,9},{11,10},{12... | collective-permute-start | bytes 12296 | tf_op jit(solution)/shard_map/ppermute | solution.py:21
  233.0 6.0 %collective-permute-start.8 = (f32[8,384]{1,0:T(8,128)S(1)}, f32[8,384]{1,0:T(8,128)S(1)}, u32[]{:S(2)}, u32[]{:S(2)}) collective-permute-start(f32[8,384]{1,0:T(8,128)S(1)} %get-tuple-element.74), channel_id=1, source_target_pairs={{8,0},{16,8},{24,16},{32,24},{40,32},{48,40},{56,48},{64,56},{72,6... | collective-permute-start | bytes 36872 | tf_op jit(solution)/shard_map/ppermute | solution.py:21
  244.6 5.5 %add_divide_fusion.1 = f32[8,128,384]{1,2,0:T(8,128)S(1)} fusion(f32[8,128,384]{1,2,0:T(8,128)S(1)} %add_divide_fusion.2, f32[8,128,383]{1,2,0:T(8,128)} %get-tuple-element.99, f32[8,128,1]{1,2,0:T(1,128)S(1)} %bitcast.767, f32[8,128,1]{1,2,0:T(1,128)S(1)} %bitcast.769, f32[8,128,383]{1,2,0:T(8,128)} %get-tuple-element.98, ...), kind=kLoop, calls=%fused_computation.42 | loop fusion | flops 9437184 | bytes 12780096 | tf_op jit(solution)/shard_map/div | solution.py:148
  254.7 3.6 %collective-permute-start.14 = (f32[8,128]{1,0:T(8,128)S(1)}, f32[8,128]{1,0:T(8,128)S(1)}, u32[]{:S(2)}, u32[]{:S(2)}) collective-permute-start(f32[8,128]{1,0:T(8,128)S(1)} %bitcast.772), channel_id=1, source_target_pairs={{1,0},{2,1},{3,2},{4,3},{5,4},{6,5},{7,6},{9,8},{10,9},{11,10},{12... | collective-permute-start | bytes 12296 | tf_op jit(solution)/shard_map/ppermute | solution.py:21
  260.3 6.0 %collective-permute-start.12 = (f32[8,384]{1,0:T(8,128)S(1)}, f32[8,384]{1,0:T(8,128)S(1)}, u32[]{:S(2)}, u32[]{:S(2)}) collective-permute-start(f32[8,384]{1,0:T(8,128)S(1)} %get-tuple-element.72), channel_id=1, source_target_pairs={{8,0},{16,8},{24,16},{32,24},{40,32},{48,40},{56,48},{64,56},{72,6... | collective-permute-start | bytes 36872 | tf_op jit(solution)/shard_map/ppermute | solution.py:21
  272.0 5.9 %add_divide_fusion = f32[8,128,384]{1,2,0:T(8,128)} fusion(f32[8,128,384]{1,2,0:T(8,128)S(1)} %add_divide_fusion.1, f32[8,128,383]{1,2,0:T(8,128)} %get-tuple-element.93, f32[8,128,1]{1,2,0:T(1,128)S(1)} %bitcast.764, f32[8,128,1]{1,2,0:T(1,128)S(1)} %bitcast.765, f32[8,128,383]{1,2,0:T(8,128)S(1)} %get-tuple-element.92, ...), kind=kLoop, calls=%fused_computation.41 | loop fusion | flops 9043968 | bytes 12780096 | tf_op jit(solution)/shard_map/div | solution.py:148
  277.9 3.0 %copy.4966 = f32[8,128,384]{2,1,0:T(8,128)} copy(f32[8,128,384]{1,2,0:T(8,128)} %add_divide_fusion) | data formatting | bytes 3145728
  (239 shorter events, 148.7 us)
Async XLA Ops:
  2.3 47.8 %collective-permute-start.3 = (f32[8,128]{1,0:T(8,128)S(1)}, f32[8,128]{1,0:T(8,128)S(1)}, u32[]{:S(2)}, u32[]{:S(2)}) collective-permute-start(f32[8,128]{1,0:T(8,128)S(1)} %get-tuple-element.71), channel_id=1, source_target_pairs={{0,1},{1,2},{2,3},{3,4},{4,5},{5,6},{6,7},{8,9},{9,10},{10,11},{11... | collective-permute-start | bytes 12296 | tf_op jit(solution)/shard_map/ppermute | solution.py:21
  4.3 46.1 %collective-permute-start.2 = (f32[8,128]{1,0:T(8,128)S(1)}, f32[8,128]{1,0:T(8,128)S(1)}, u32[]{:S(2)}, u32[]{:S(2)}) collective-permute-start(f32[8,128]{1,0:T(8,128)S(1)} %get-tuple-element.70), channel_id=1, source_target_pairs={{1,0},{2,1},{3,2},{4,3},{5,4},{6,5},{7,6},{9,8},{10,9},{11,10},{12... | collective-permute-start | bytes 12296 | tf_op jit(solution)/shard_map/ppermute | solution.py:21
  8.9 41.7 %collective-permute-start.1 = (f32[8,512]{1,0:T(8,128)S(1)}, f32[8,512]{1,0:T(8,128)S(1)}, u32[]{:S(2)}, u32[]{:S(2)}) collective-permute-start(f32[8,512]{1,0:T(8,128)S(1)} %bitcast.752), channel_id=1, source_target_pairs={{0,8},{8,16},{16,24},{24,32},{32,40},{40,48},{48,56},{56,64},{64,7... | collective-permute-start | bytes 49160 | tf_op jit(solution)/shard_map/ppermute | solution.py:21
  12.3 38.3 %collective-permute-start = (f32[8,512]{1,0:T(8,128)S(1)}, f32[8,512]{1,0:T(8,128)S(1)}, u32[]{:S(2)}, u32[]{:S(2)}) collective-permute-start(f32[8,512]{1,0:T(8,128)S(1)} %bitcast.754), channel_id=1, source_target_pairs={{8,0},{16,8},{24,16},{32,24},{40,32},{48,40},{56,48},{64,56},{72,6... | collective-permute-start | bytes 49160 | tf_op jit(solution)/shard_map/ppermute | solution.py:21
  20.4 8.5 %copy-start = (f32[8,128,512]{2,1,0:T(8,128)S(1)}, f32[8,128,512]{2,1,0:T(8,128)}, u32[]{:S(2)}) copy-start(f32[8,128,512]{2,1,0:T(8,128)} %param.9) | copy-start | bytes 6291460
  20.4 50.0 %all-to-all-start = ((f32[8,128,384]{2,0,1:T(8,128)}), f32[8,128,384]{2,0,1:T(8,128)}, u32[]{:S(2)}, u32[]{:S(2)}) async-start(f32[8,128,384]{2,0,1:T(8,128)} %copy.4947), calls=%async_computation | async-start | bytes 3145728 | tf_op jit(solution)/shard_map/all_to_all | solution.py:49
  35.0 2.6 copy-start.4
  35.0 4.0 %copy-start.5 = (s32[16384]{0:T(1024)S(1)}, s32[16384]{0:T(1024)}, u32[]{:S(2)}) copy-start(s32[16384]{0:T(1024)} %param.16) | copy-start | bytes 196612
  35.0 4.8 %copy-start.7 = (s32[2,4]{1,0:T(2,128)S(1)}, s32[2,4]{1,0:T(2,128)}, u32[]{:S(2)}) copy-start(s32[2,4]{1,0:T(2,128)} %param.17) | copy-start | bytes 100
  70.4 90.1 %all-to-all-start.2 = ((f32[128,2,2048]{2,1,0:T(2,128)}), f32[128,2,2048]{2,1,0:T(2,128)S(1)}, u32[]{:S(2)}, u32[]{:S(2)}) async-start(f32[128,2,2048]{2,1,0:T(2,128)} %copy.4959), calls=%async_computation.2 | async-start | bytes 4194304 | tf_op jit(solution)/shard_map/all_to_all | solution.py:123
  160.5 10.4 %copy-start.3 = (bf16[128,384]{1,0:T(8,128)(2,1)S(1)}, bf16[128,384]{1,0:T(8,128)(2,1)}, u32[]{:S(2)}) copy-start(bf16[128,384]{1,0:T(8,128)(2,1)} %param.12) | copy-start | bytes 294916
  160.5 31.5 %all-to-all-start.1 = ((f32[128,8,1,384]{3,1,2,0:T(8,128)}), f32[128,8,1,384]{3,1,2,0:T(8,128)}, u32[]{:S(2)}, u32[]{:S(2)}) async-start(f32[128,8,1,384]{3,1,2,0:T(8,128)} %constant_dynamic-update-slice_fusion), calls=%async_computation.1 | async-start | bytes 3145728 | tf_op jit(solution)/shard_map/all_to_all | solution.py:55
  197.1 19.6 %collective-permute-start.7 = (f32[8,128]{1,0:T(8,128)S(1)}, f32[8,128]{1,0:T(8,128)S(1)}, u32[]{:S(2)}, u32[]{:S(2)}) collective-permute-start(f32[8,128]{1,0:T(8,128)S(1)} %bitcast.773), channel_id=1, source_target_pairs={{0,1},{1,2},{2,3},{3,4},{4,5},{5,6},{6,7},{8,9},{9,10},{10,11},{11... | collective-permute-start | bytes 12296 | tf_op jit(solution)/shard_map/ppermute | solution.py:21
  199.1 17.7 %collective-permute-start.6 = (f32[8,128]{1,0:T(8,128)S(1)}, f32[8,128]{1,0:T(8,128)S(1)}, u32[]{:S(2)}, u32[]{:S(2)}) collective-permute-start(f32[8,128]{1,0:T(8,128)S(1)} %bitcast.770), channel_id=1, source_target_pairs={{1,0},{2,1},{3,2},{4,3},{5,4},{6,5},{7,6},{9,8},{10,9},{11,10},{12... | collective-permute-start | bytes 12296 | tf_op jit(solution)/shard_map/ppermute | solution.py:21
  202.9 10.4 %collective-permute-start.5 = (f32[8,384]{1,0:T(8,128)S(1)}, f32[8,384]{1,0:T(8,128)S(1)}, u32[]{:S(2)}, u32[]{:S(2)}) collective-permute-start(f32[8,384]{1,0:T(8,128)S(1)} %get-tuple-element.77), channel_id=1, source_target_pairs={{0,8},{8,16},{16,24},{24,32},{32,40},{40,48},{48,56},{56,64},{64,7... | collective-permute-start | bytes 36872 | tf_op jit(solution)/shard_map/ppermute | solution.py:21
  205.7 9.4 %collective-permute-start.4 = (f32[8,384]{1,0:T(8,128)S(1)}, f32[8,384]{1,0:T(8,128)S(1)}, u32[]{:S(2)}, u32[]{:S(2)}) collective-permute-start(f32[8,384]{1,0:T(8,128)S(1)} %get-tuple-element.76), channel_id=1, source_target_pairs={{8,0},{16,8},{24,16},{32,24},{40,32},{48,40},{56,48},{64,56},{72,6... | collective-permute-start | bytes 36872 | tf_op jit(solution)/shard_map/ppermute | solution.py:21
  225.5 19.1 %collective-permute-start.11 = (f32[8,128]{1,0:T(8,128)S(1)}, f32[8,128]{1,0:T(8,128)S(1)}, u32[]{:S(2)}, u32[]{:S(2)}) collective-permute-start(f32[8,128]{1,0:T(8,128)S(1)} %bitcast.774), channel_id=1, source_target_pairs={{0,1},{1,2},{2,3},{3,4},{4,5},{5,6},{6,7},{8,9},{9,10},{10,11},{11... | collective-permute-start | bytes 12296 | tf_op jit(solution)/shard_map/ppermute | solution.py:21
  227.4 17.2 %collective-permute-start.10 = (f32[8,128]{1,0:T(8,128)S(1)}, f32[8,128]{1,0:T(8,128)S(1)}, u32[]{:S(2)}, u32[]{:S(2)}) collective-permute-start(f32[8,128]{1,0:T(8,128)S(1)} %bitcast.771), channel_id=1, source_target_pairs={{1,0},{2,1},{3,2},{4,3},{5,4},{6,5},{7,6},{9,8},{10,9},{11,10},{12... | collective-permute-start | bytes 12296 | tf_op jit(solution)/shard_map/ppermute | solution.py:21
  231.0 10.1 %collective-permute-start.9 = (f32[8,384]{1,0:T(8,128)S(1)}, f32[8,384]{1,0:T(8,128)S(1)}, u32[]{:S(2)}, u32[]{:S(2)}) collective-permute-start(f32[8,384]{1,0:T(8,128)S(1)} %get-tuple-element.75), channel_id=1, source_target_pairs={{0,8},{8,16},{16,24},{24,32},{32,40},{40,48},{48,56},{56,64},{64,7... | collective-permute-start | bytes 36872 | tf_op jit(solution)/shard_map/ppermute | solution.py:21
  233.0 9.9 %collective-permute-start.8 = (f32[8,384]{1,0:T(8,128)S(1)}, f32[8,384]{1,0:T(8,128)S(1)}, u32[]{:S(2)}, u32[]{:S(2)}) collective-permute-start(f32[8,384]{1,0:T(8,128)S(1)} %get-tuple-element.74), channel_id=1, source_target_pairs={{8,0},{16,8},{24,16},{32,24},{40,32},{48,40},{56,48},{64,56},{72,6... | collective-permute-start | bytes 36872 | tf_op jit(solution)/shard_map/ppermute | solution.py:21
  252.8 19.2 %collective-permute-start.15 = (f32[8,128]{1,0:T(8,128)S(1)}, f32[8,128]{1,0:T(8,128)S(1)}, u32[]{:S(2)}, u32[]{:S(2)}) collective-permute-start(f32[8,128]{1,0:T(8,128)S(1)} %bitcast.775), channel_id=1, source_target_pairs={{0,1},{1,2},{2,3},{3,4},{4,5},{5,6},{6,7},{8,9},{9,10},{10,11},{11... | collective-permute-start | bytes 12296 | tf_op jit(solution)/shard_map/ppermute | solution.py:21
  254.7 17.2 %collective-permute-start.14 = (f32[8,128]{1,0:T(8,128)S(1)}, f32[8,128]{1,0:T(8,128)S(1)}, u32[]{:S(2)}, u32[]{:S(2)}) collective-permute-start(f32[8,128]{1,0:T(8,128)S(1)} %bitcast.772), channel_id=1, source_target_pairs={{1,0},{2,1},{3,2},{4,3},{5,4},{6,5},{7,6},{9,8},{10,9},{11,10},{12... | collective-permute-start | bytes 12296 | tf_op jit(solution)/shard_map/ppermute | solution.py:21
  258.4 10.2 %collective-permute-start.13 = (f32[8,384]{1,0:T(8,128)S(1)}, f32[8,384]{1,0:T(8,128)S(1)}, u32[]{:S(2)}, u32[]{:S(2)}) collective-permute-start(f32[8,384]{1,0:T(8,128)S(1)} %get-tuple-element.73), channel_id=1, source_target_pairs={{0,8},{8,16},{16,24},{24,32},{32,40},{40,48},{48,56},{56,64},{64,7... | collective-permute-start | bytes 36872 | tf_op jit(solution)/shard_map/ppermute | solution.py:21
  260.3 9.9 %collective-permute-start.12 = (f32[8,384]{1,0:T(8,128)S(1)}, f32[8,384]{1,0:T(8,128)S(1)}, u32[]{:S(2)}, u32[]{:S(2)}) collective-permute-start(f32[8,384]{1,0:T(8,128)S(1)} %get-tuple-element.72), channel_id=1, source_target_pairs={{8,0},{16,8},{24,16},{32,24},{40,32},{48,40},{56,48},{64,56},{72,6... | collective-permute-start | bytes 36872 | tf_op jit(solution)/shard_map/ppermute | solution.py:21
  (3 other events, 6.6 us)
